TPU v7x, 512 devices: a whole 4x4x16 slice. The times are simulated.
512 devices in a mesh: pipe: 16 (over z_hi, x, core), tensor: 32 (over z_lo, y).
Axes of the slice: x: 4, y: 4, z: 16 (z_hi: 2, z_lo: 8; z = z_hi * 8 + z_lo), core: 2. Of those that a mesh axis runs over, the one named last changes fastest.
Arguments:
- tokens: bfloat16 [512, 8192], P(None, 'pipe'), may hold values from -6 to 6
- out_grad: bfloat16 [512, 8192], P(None, 'pipe'), may hold values from -6 to 6
- w_gate: bfloat16 [8192, 16384], P('pipe', 'tensor'), may hold values from -0.0625 to 0.0625
- w_up: bfloat16 [8192, 16384], P('pipe', 'tensor'), may hold values from -0.0625 to 0.0625
- w_down: bfloat16 [16384, 8192], P('tensor', 'pipe'), may hold values from -0.046875 to 0.046875
Outputs:
- input_grad: float32 [512, 8192], P('tensor', 'pipe')
- gate_mantissa: bfloat16 [8192, 16384], P('pipe', 'tensor')
- gate_scales: float32 [256, 8192], P('pipe', 'tensor')
- up_mantissa: bfloat16 [8192, 16384], P('pipe', 'tensor')
- up_scales: float32 [256, 8192], P('pipe', 'tensor')
- down_mantissa: bfloat16 [16384, 8192], P('tensor', 'pipe')
- down_scales: float32 [8192, 256], P('tensor', 'pipe')
All inputs are finite; a program needn't handle non-finite values.
Results may differ from a plain program's by a relative error of at most 0.0049.
Values may be sent and summed in bfloat16 or wider, within the bound.
No kernel may reach another device: no remote copies, remote signals or barrier semaphores. Data moves between devices by JAX's collectives and lax.ppermute only.
A program may use at most 64 MiB of HBM per device.

v0:
```python
import jax
import jax.numpy as jnp
import numpy as np
from jax import lax
from jax.sharding import Mesh
from jax.sharding import PartitionSpec as P

PIPE_MODE = "hier"
TENSOR_MODE = "zlo_y"
PIPE = ("z_hi", "x", "core")
TENSOR = ("z_lo", "y")


def quantize_features(grad):
    rows, cols = grad.shape
    blocks = grad.reshape(rows // 32, 32, cols // 2, 2)
    scales = jnp.max(jnp.abs(blocks), axis=(1, 3)) + 1e-06
    mantissa = (blocks / scales[:, None, :, None]).reshape(grad.shape)
    return (mantissa.astype(jnp.bfloat16), scales)


def quantize_hidden(grad):
    rows, cols = grad.shape
    blocks = grad.reshape(rows // 2, 2, cols // 32, 32)
    scales = jnp.max(jnp.abs(blocks), axis=(1, 3)) + 1e-06
    mantissa = (blocks / scales[:, None, :, None]).reshape(grad.shape)
    return (mantissa.astype(jnp.bfloat16), scales)


def contract_last(left, right):
    return lax.dot_general(
        left, right, (((1,), (1,)), ((), ())), preferred_element_type=jnp.float32
    )


def contract_first(left, right):
    return lax.dot_general(
        left, right, (((0,), (0,)), ((), ())), preferred_element_type=jnp.float32
    )


def gate_terms(gate, up, hidden_grad):
    sigmoid_gate = jax.nn.sigmoid(gate)
    silu_gate = gate * sigmoid_gate
    hidden = (silu_gate * up).astype(jnp.bfloat16)
    gate_grad = (hidden_grad * up * sigmoid_gate * (1.0 + gate * (1.0 - sigmoid_gate))).astype(
        jnp.bfloat16
    )
    up_grad = (hidden_grad * silu_gate).astype(jnp.bfloat16)
    return (hidden, gate_grad, up_grad)


def pipe_exchange(parts):
    if PIPE_MODE == "flat_ar":
        gate, up, hidden_grad = lax.psum(tuple(parts), PIPE)
        return gate_terms(gate, up, hidden_grad)
    stacked = jnp.stack(parts)
    if PIPE_MODE == "flat":
        shard = lax.psum_scatter(stacked, PIPE, scatter_dimension=1, tiled=True)
    else:
        shard = stacked
        for axis in ("core", "x", "z_hi"):
            shard = lax.psum_scatter(shard, axis, scatter_dimension=1, tiled=True)
    products = jnp.stack(gate_terms(shard[0], shard[1], shard[2]))
    if PIPE_MODE == "flat":
        full = lax.all_gather(products, PIPE, axis=1, tiled=True)
    else:
        full = products
        for axis in ("z_hi", "x", "core"):
            full = lax.all_gather(full, axis, axis=1, tiled=True)
    return (full[0], full[1], full[2])


def tensor_exchange(partial, n_zlo, n_y):
    if TENSOR_MODE == "flat":
        return lax.psum_scatter(partial, TENSOR, scatter_dimension=0, tiled=True)
    if TENSOR_MODE == "zlo_y":
        partial = lax.psum_scatter(partial, "z_lo", scatter_dimension=0, tiled=True)
        return lax.psum_scatter(partial, "y", scatter_dimension=0, tiled=True)
    rows, cols = partial.shape
    blocks = partial.reshape(n_zlo, n_y, rows // (n_zlo * n_y), cols)
    blocks = jnp.swapaxes(blocks, 0, 1).reshape(rows, cols)
    blocks = lax.psum_scatter(blocks, "y", scatter_dimension=0, tiled=True)
    return lax.psum_scatter(blocks, "z_lo", scatter_dimension=0, tiled=True)


def make_on_device(n_zlo, n_y):

    def on_device(tokens, out_grad, w_gate, w_up, w_down):
        gate_part = jnp.dot(tokens, w_gate, preferred_element_type=jnp.float32)
        up_part = jnp.dot(tokens, w_up, preferred_element_type=jnp.float32)
        hidden_part = contract_last(out_grad, w_down)
        hidden, gate_grad, up_grad = pipe_exchange((gate_part, up_part, hidden_part))
        input_grad = tensor_exchange(
            contract_last(gate_grad, w_gate) + contract_last(up_grad, w_up), n_zlo, n_y
        )
        gate_mantissa, gate_scales = quantize_features(contract_first(tokens, gate_grad))
        up_mantissa, up_scales = quantize_features(contract_first(tokens, up_grad))
        down_mantissa, down_scales = quantize_hidden(contract_first(hidden, out_grad))
        return (
            input_grad,
            gate_mantissa,
            gate_scales,
            up_mantissa,
            up_scales,
            down_mantissa,
            down_scales,
        )

    return on_device


def fine_mesh(mesh):
    n_pipe, n_tensor = (mesh.shape["pipe"], mesh.shape["tensor"])
    n_y = 4
    n_zlo = n_tensor // n_y
    n_core = 2
    n_x = 4
    n_zhi = n_pipe // (n_core * n_x)
    devices = np.asarray(mesh.devices).reshape(n_zhi, n_x, n_core, n_zlo, n_y)
    return (Mesh(devices, ("z_hi", "x", "core", "z_lo", "y")), n_zlo, n_y)


def solution(mesh):
    fine, n_zlo, n_y = fine_mesh(mesh)
    in_specs = (P(None, PIPE), P(None, PIPE), P(PIPE, TENSOR), P(PIPE, TENSOR), P(TENSOR, PIPE))
    out_specs = (
        P(TENSOR, PIPE),
        P(PIPE, TENSOR),
        P(PIPE, TENSOR),
        P(PIPE, TENSOR),
        P(PIPE, TENSOR),
        P(TENSOR, PIPE),
        P(TENSOR, PIPE),
    )
    return jax.shard_map(
        make_on_device(n_zlo, n_y),
        mesh=fine,
        in_specs=in_specs,
        out_specs=out_specs,
        check_vma=False,
    )
```

profile of v0, /device:TPU:6, one launch (start us, length us, event | category | flops | bytes accessed | tf_op | source)
XLA Modules:
  0.0 276.1 jit_solution(17815208416039630571)
XLA Ops:
  7.2 0.0 copy-start
  7.2 0.0 copy-start.5
  7.2 0.0 copy-start.4
  7.2 0.0 copy-start.8
  7.2 0.0 reduce-scatter.6.cloned.1.call-start
  7.3 1.0 copy-done
  8.2 1.5 convolution_bitcast_fusion.3
  9.7 0.0 copy-done.5
  9.7 0.4 convolution_bitcast_fusion.4
  10.1 0.0 copy-done.4
  10.1 0.0 copy-done.8
  10.2 0.5 convolution_bitcast_fusion.2
  10.6 1.9 pad_maximum_fusion
  12.6 0.0 reduce-scatter.6.cloned.1.call-update
  12.6 0.0 reduce-scatter.8.cloned.1.call-start
  12.6 26.1 %reduce-scatter.6.cloned.1.call-done = f32[3,256,512]{2,1,0:T(8,128)} async-done(((f32[3,512,512]{2,1,0:T(8,128)}), f32[3,256,512]{2,1,0:T(8,128)}) %reduce-scatter.6.cloned.1.call-update) | async-done | bytes 1572880 | tf_op jit(solution)/shard_map/reduce_scatter | solution.py:63
  38.7 0.0 reduce-scatter.8.cloned.1.call-update
  38.8 0.0 reduce-scatter.10.cloned.1.call-start
  38.8 36.7 %reduce-scatter.8.cloned.1.call-done = f32[3,64,512]{2,1,0:T(8,128)} async-done(((f32[3,256,512]{2,1,0:T(8,128)}), f32[3,64,512]{2,1,0:T(8,128)}) %reduce-scatter.8.cloned.1.call-update) | async-done | bytes 393232 | tf_op jit(solution)/shard_map/reduce_scatter | solution.py:63
  75.5 0.0 reduce-scatter.10.cloned.1.call-update
  75.5 0.0 all-gather.2.cloned.1.call-start
  75.6 48.8 %reduce-scatter.10.cloned.1.call-done = f32[3,32,512]{2,1,0:T(8,128)} async-done(((f32[3,64,512]{2,1,0:T(8,128)}), f32[3,32,512]{2,1,0:T(8,128)}) %reduce-scatter.10.cloned.1.call-update) | async-done | bytes 196624 | tf_op jit(solution)/shard_map/reduce_scatter | solution.py:63
  124.3 0.9 multiply_convert_fusion.2
  125.3 17.1 %all_gather.9 = bf16[3,64,512]{2,1,0:T(8,128)(2,1)S(1)} all-gather(bf16[3,32,512]{2,1,0:T(8,128)(2,1)S(1)} %pad_maximum_fusion.1), channel_id=1, replica_groups=mesh['z_hi'=2,'x'=4,'core'=2,'z_lo'=8,'y'=4] {'z_hi'}, dimensions={1}, use_global_device_ids=true | all-gather | bytes 294912 | tf_op jit(solution)/shard_map/all_gather | solution.py:70
  142.4 15.0 %all_gather.10 = bf16[3,256,512]{2,1,0:T(8,128)(2,1)} all-gather(bf16[3,64,512]{2,1,0:T(8,128)(2,1)S(1)} %all_gather.9), channel_id=1, replica_groups=mesh['z_hi'=2,'x'=4,'core'=2,'z_lo'=8,'y'=4] {'x'}, dimensions={1}, use_global_device_ids=true | all-gather | bytes 983040 | tf_op jit(solution)/shard_map/all_gather | solution.py:70
  157.4 0.0 all-gather.2.cloned.1.call-update
  157.4 0.0 reduce-scatter.12.cloned.1.call-start
  157.5 1.0 copy.27
  158.5 12.8 %all-gather.2.cloned.1.call-done = bf16[3,512,512]{2,1,0:T(8,128)(2,1)} async-done(((bf16[3,256,512]{2,1,0:T(8,128)(2,1)}), bf16[3,512,512]{2,1,0:T(8,128)(2,1)}) %all-gather.2.cloned.1.call-update) | async-done | bytes 1572880 | tf_op jit(solution)/shard_map/all_gather | solution.py:70
  171.3 1.6 fusion.2
  172.9 0.0 copy-done.6
  172.9 0.0 copy-done.1
  172.9 1.4 convolution_add_fusion
  174.4 0.0 reduce-scatter.12.cloned.1.call-update
  174.4 0.2 reduce-scatter.14.cloned.1.call-start
  174.6 1.5 fusion.4
  176.1 2.5 abs.16
  178.6 2.8 %reduce_max.27 = f32[16,256]{0,1:T(8,128)S(1)} reduce(f32[16,32,256,2]{1,0,3,2:T(8,128)} %abs.16, f32[]{:T(128)} %constant.0.clone.1), dimensions={1,3}, to_apply=%region_5.0 | reduce | flops 258048 | bytes 1064964 | tf_op jit(solution)/shard_map/reduce_max | solution.py:17
  181.4 0.7 copy.31
  182.1 2.5 div.37
  184.7 4.5 %div.38 = f32[512,512]{0,1:T(8,128)} reshape(f32[16,32,256,2]{1,0,3,2:T(8,128)} %div.37) | data formatting | bytes 2097152 | tf_op jit(solution)/shard_map/div | solution.py:18
  189.1 0.0 copy-done.3
  189.1 2.2 divide_convert_fusion.2
  191.4 2.1 copy.30
  193.4 1.5 fusion.5
  194.9 2.5 abs.18
  197.4 2.8 %reduce_max.28 = f32[16,256]{0,1:T(8,128)S(1)} reduce(f32[16,32,256,2]{1,0,3,2:T(8,128)} %abs.18, f32[]{:T(128)} %constant.0.clone.1), dimensions={1,3}, to_apply=%region_6.0 | reduce | flops 258048 | bytes 1064964 | tf_op jit(solution)/shard_map/reduce_max | solution.py:17
  200.2 0.7 copy.33
  200.9 2.5 div.40
  203.4 4.5 %div.41 = f32[512,512]{0,1:T(8,128)} reshape(f32[16,32,256,2]{1,0,3,2:T(8,128)} %div.40) | data formatting | bytes 2097152 | tf_op jit(solution)/shard_map/div | solution.py:18
  207.9 0.0 copy-done.2
  207.9 2.2 divide_convert_fusion.1
  210.1 2.1 copy.32
  212.3 0.2 copy.26
  212.5 0.2 dot_general.46
  212.7 0.0 copy-done.7
  212.7 0.5 abs_reduce_fusion
  213.2 0.0 copy-start.9
  213.2 30.7 %reduce-scatter.12.cloned.1.call-done = f32[64,512]{1,0:T(8,128)} async-done(((f32[512,512]{1,0:T(8,128)}), f32[64,512]{1,0:T(8,128)}) %reduce-scatter.12.cloned.1.call-update) | async-done | bytes 131088 | tf_op jit(solution)/shard_map/reduce_scatter | solution.py:78
  243.9 0.0 reduce-scatter.14.cloned.1.call-update
  243.9 0.1 divide_convert_fusion
  244.0 3.0 %copy.29 = bf16[256,2,16,32]{3,2,1,0:T(8,128)(2,1)S(1)} copy(bf16[256,2,16,32]{0,3,2,1:T(8,128)(2,1)S(1)} %divide_convert_fusion) | data formatting | bytes 1048576 | tf_op jit(solution)/shard_map/convert_element_type | solution.py:27
  247.1 2.8 convert_element_type.30
  249.8 19.5 %reduce-scatter.14.cloned.1.call-done = f32[16,512]{1,0:T(8,128)} async-done(((f32[64,512]{1,0:T(8,128)}), f32[16,512]{1,0:T(8,128)}) %reduce-scatter.14.cloned.1.call-update) | async-done | bytes 32784 | tf_op jit(solution)/shard_map/reduce_scatter | solution.py:79
  (11 shorter events, 0.1 us)
Async XLA Ops:
  7.2 1.0 copy-start
  7.2 2.5 copy-start.5
  7.2 2.9 %copy-start.4 = (bf16[512,512]{1,0:T(8,128)(2,1)S(1)}, bf16[512,512]{1,0:T(8,128)(2,1)}, u32[]{:S(2)}) copy-start(bf16[512,512]{1,0:T(8,128)(2,1)} %param.6) | copy-start | bytes 1572868
  7.2 2.9 %copy-start.8 = (bf16[512,512]{1,0:T(8,128)(2,1)S(1)}, bf16[512,512]{1,0:T(8,128)(2,1)}, u32[]{:S(2)}) copy-start(bf16[512,512]{1,0:T(8,128)(2,1)} %param.9) | copy-start | bytes 1572868
  7.2 31.5 %reduce-scatter.6.cloned.1.call-start = ((), (), s32[]{:S(2)}) async-start(), calls=%async_computation.5 | async-start | bytes 4718592 | tf_op jit(solution)/shard_map/reduce_scatter | solution.py:63
  12.6 62.9 %reduce-scatter.8.cloned.1.call-start = ((), (), s32[]{:S(2)}) async-start(), calls=%async_computation.6 | async-start | bytes 1966080 | tf_op jit(solution)/shard_map/reduce_scatter | solution.py:63
  38.8 85.5 %reduce-scatter.10.cloned.1.call-start = ((), (), s32[]{:S(2)}) async-start(), calls=%async_computation.7 | async-start | bytes 589824 | tf_op jit(solution)/shard_map/reduce_scatter | solution.py:63
  75.5 95.8 %all-gather.2.cloned.1.call-start = ((), (), s32[]{:S(2)}) async-start(), calls=%async_computation.8 | async-start | bytes 2359296 | tf_op jit(solution)/shard_map/all_gather | solution.py:70
  157.4 15.5 %copy-start.6 = (bf16[512,512]{1,0:T(8,128)(2,1)S(1)}, bf16[512,512]{1,0:T(8,128)(2,1)}, u32[]{:S(2)}) copy-start(bf16[512,512]{1,0:T(8,128)(2,1)} %param.8) | copy-start | bytes 1572868
  157.4 86.5 %reduce-scatter.12.cloned.1.call-start = ((), (), s32[]{:S(2)}) async-start(), calls=%async_computation.9 | async-start | bytes 1179648 | tf_op jit(solution)/shard_map/reduce_scatter | solution.py:78
  171.3 1.6 copy-start.1
  174.4 94.9 %reduce-scatter.14.cloned.1.call-start = ((), (), s32[]{:S(2)}) async-start(), calls=%async_computation.10 | async-start | bytes 163840 | tf_op jit(solution)/shard_map/reduce_scatter | solution.py:79
  184.7 4.5 %copy-start.3 = (f32[512,512]{0,1:T(8,128)S(1)}, f32[512,512]{0,1:T(8,128)}, u32[]{:S(2)}) copy-start(f32[512,512]{0,1:T(8,128)} %get-tuple-element.32) | copy-start | bytes 3145732
  203.4 4.5 %copy-start.2 = (f32[512,512]{0,1:T(8,128)S(1)}, f32[512,512]{0,1:T(8,128)}, u32[]{:S(2)}) copy-start(f32[512,512]{0,1:T(8,128)} %get-tuple-element.34) | copy-start | bytes 3145732
  210.1 2.6 copy-start.7
  213.2 33.8 %copy-start.9 = (f32[256,16]{0,1:T(8,128)}, f32[256,16]{0,1:T(8,128)S(1)}, u32[]{:S(2)}) copy-start(f32[256,16]{0,1:T(8,128)S(1)} %broadcast_add_fusion.2) | copy-start | bytes 49156
Sparse Core Ops, SparseCore 0:
  12.7 25.9 reduce-scatter.5
  41.6 33.8 reduce-scatter.7
  78.3 45.9 reduce-scatter.9
  157.5 13.7 all-gather.1
  174.5 69.3 reduce-scatter.11
  247.1 22.1 reduce-scatter.13
where the time goes:
time: 277 us; the launch traced here: 276 us
  waiting for transfers between devices  175 us (63%)
  local copies, waits for them, and re-layouts  32.7 us (12%)
  blocking collectives  32.1 us (12%)
  between operations  14.3 us (5%)
  other arithmetic  13.1 us (5%)
  matrix products  8.85 us (3%)
    reduce_scatter x3, waiting for transfers between devices, pipe_exchange(): shard = lax.psum_scatter(shard, axis, scatter_dimension=1, tiled=True)  112 us
    all_gather x2, blocking collectives, pipe_exchange(): full = lax.all_gather(full, axis, axis=1, tiled=True)  32.1 us
    reduce_scatter x1, waiting for transfers between devices, tensor_exchange(): partial = lax.psum_scatter(partial, 'z_lo', scatter_dimension=0, tiled=True)  30.7 us
    reduce_scatter x1, waiting for transfers between devices, tensor_exchange(): return lax.psum_scatter(partial, 'y', scatter_dimension=0, tiled=True)  19.5 us
    div x4, local copies, waits for them, and re-layouts, quantize_features(): mantissa = (blocks / scales[:, None, :, None]).reshape(grad.shape)  14.1 us
    all_gather x1, waiting for transfers between devices, pipe_exchange(): full = lax.all_gather(full, axis, axis=1, tiled=True)  12.8 us
    unnamed x25, local copies, waits for them, and re-layouts  7.51 us
    convert_element_type x2, local copies, waits for them, and re-layouts, quantize_hidden(): return (mantissa.astype(jnp.bfloat16), scales)  5.76 us
  transfers between devices with their start and end apart: 6, of which 6 were waited for; matrix products, arithmetic and copies ran while one was open for 16% of the time, Pallas kernels for 0%

commit v1 on v0

--- a/solution.py
+++ b/solution.py
@@ -67,7 +67,19 @@
     else:
         full = products
         for axis in ("z_hi", "x", "core"):
-            full = lax.all_gather(full, axis, axis=1, tiled=True)
+
+            def _direct_vector(my_tile):
+                return jnp.concatenate(
+                    jax.lax.all_to_all(
+                        jnp.stack([my_tile for _ in range(jax.lax.axis_size(axis))], axis=0),
+                        axis,
+                        0,
+                        0,
+                    ),
+                    axis=1,
+                )
+
+            full = _direct_vector(full)
     return (full[0], full[1], full[2])
 
 

time: 277 us -> 266 us (0.960)
  blocking collectives: 32.1 us -> 23.1 us
  starting transfers between devices: 0.42 us -> 5.14 us
  waiting for transfers between devices: 175 us -> 171 us
  other arithmetic: 13.1 us -> 10.1 us
    all_gather x2 -> x0, blocking collectives: 32.1 us -> none  [pipe_exchange(): full = lax.all_gather(full, axis, axis=1, tiled=True)]
    all_to_all x0 -> x2, blocking collectives: none -> 23.1 us  [_direct_vector(): jax.lax.all_to_all(jnp.stack([my_tile for _ in range(jax.lax.axis_size(ax...]
    all_gather x1 -> x0, waiting for transfers between devices: 12.8 us -> none  [pipe_exchange(): full = lax.all_gather(full, axis, axis=1, tiled=True)]
    all_to_all x0 -> x1, waiting for transfers between devices: none -> 6.4 us  [_direct_vector(): jax.lax.all_to_all(jnp.stack([my_tile for _ in range(jax.lax.axis_size(ax...]
    all_to_all x0 -> x1, starting transfers between devices: none -> 4.8 us  [_direct_vector(): jax.lax.all_to_all(jnp.stack([my_tile for _ in range(jax.lax.axis_size(ax...]
    reduce_scatter x1, waiting for transfers between devices: 30.7 us -> 34.2 us  [tensor_exchange(): partial = lax.psum_scatter(partial, 'z_lo', scatter_dimension=0, tiled=True)]
    convert_element_type x2, other arithmetic: 4.43 us -> 1.24 us  [quantize_features(): return (mantissa.astype(jnp.bfloat16), scales)]
    unnamed x25 -> x19, local copies, waits for them, and re-layouts: 7.51 us -> 6.42 us
  transfers between devices with their start and end apart: 6 -> 6, of which waited for: 6 -> 6; matrix products, arithmetic and copies ran while one was open for 16% -> 15% of each run, Pallas kernels for 0% -> 0%
where the time goes in v1:
time: 266 us; the launch traced here: 265 us
  waiting for transfers between devices  171 us (64%)
  local copies, waits for them, and re-layouts  32.8 us (12%)
  blocking collectives  23.1 us (9%)
  between operations  14 us (5%)
  other arithmetic  10.1 us (4%)
  matrix products  8.78 us (3%)
  starting transfers between devices  5.14 us (2%)
    reduce_scatter x3, waiting for transfers between devices, pipe_exchange(): shard = lax.psum_scatter(shard, axis, scatter_dimension=1, tiled=True)  112 us
    reduce_scatter x1, waiting for transfers between devices, tensor_exchange(): partial = lax.psum_scatter(partial, 'z_lo', scatter_dimension=0, tiled=True)  34.2 us
    all_to_all x2, blocking collectives, _direct_vector(): jax.lax.all_to_all(jnp.stack([my_tile for _ in range(jax.lax.axis_size(ax...  23.1 us
    reduce_scatter x1, waiting for transfers between devices, tensor_exchange(): return lax.psum_scatter(partial, 'y', scatter_dimension=0, tiled=True)  19.1 us
    div x4, local copies, waits for them, and re-layouts, quantize_features(): mantissa = (blocks / scales[:, None, :, None]).reshape(grad.shape)  12.3 us
    unnamed x19, local copies, waits for them, and re-layouts  6.42 us
    all_to_all x1, waiting for transfers between devices, _direct_vector(): jax.lax.all_to_all(jnp.stack([my_tile for _ in range(jax.lax.axis_size(ax...  6.4 us
    convert_element_type x2, local copies, waits for them, and re-layouts, quantize_hidden(): return (mantissa.astype(jnp.bfloat16), scales)  5.76 us
  transfers between devices with their start and end apart: 6, of which 6 were waited for; matrix products, arithmetic and copies ran while one was open for 15% of the time, Pallas kernels for 0%

profile of v1, /device:TPU:6, one launch (start us, length us, event | category | flops | bytes accessed | tf_op | source)
XLA Modules:
  0.0 265.2 jit_solution(17156080661338140297)
XLA Ops:
  7.2 0.0 copy-start
  7.2 0.0 copy-start.2
  7.2 0.0 copy-start.5
  7.2 0.0 reduce-scatter.6.cloned.1.call-start
  7.2 1.0 copy-done
  8.2 1.5 convolution_bitcast_fusion.3
  9.7 1.5 convolution_bitcast_fusion.4
  11.2 0.0 copy-done.2
  11.2 0.0 copy-done.5
  11.2 0.5 convolution_bitcast_fusion.2
  11.7 2.0 pad_maximum_fusion
  13.6 0.0 reduce-scatter.6.cloned.1.call-update
  13.6 0.0 reduce-scatter.8.cloned.1.call-start
  13.7 26.1 %reduce-scatter.6.cloned.1.call-done = f32[3,256,512]{2,1,0:T(8,128)} async-done(((f32[3,512,512]{2,1,0:T(8,128)}), f32[3,256,512]{2,1,0:T(8,128)}) %reduce-scatter.6.cloned.1.call-update) | async-done | bytes 1572880 | tf_op jit(solution)/shard_map/reduce_scatter | solution.py:63
  39.8 0.0 reduce-scatter.8.cloned.1.call-update
  39.8 0.0 reduce-scatter.10.cloned.1.call-start
  39.9 36.7 %reduce-scatter.8.cloned.1.call-done = f32[3,64,512]{2,1,0:T(8,128)} async-done(((f32[3,256,512]{2,1,0:T(8,128)}), f32[3,64,512]{2,1,0:T(8,128)}) %reduce-scatter.8.cloned.1.call-update) | async-done | bytes 393232 | tf_op jit(solution)/shard_map/reduce_scatter | solution.py:63
  76.5 0.0 reduce-scatter.10.cloned.1.call-update
  76.6 48.8 %reduce-scatter.10.cloned.1.call-done = f32[3,32,512]{2,1,0:T(8,128)} async-done(((f32[3,64,512]{2,1,0:T(8,128)}), f32[3,32,512]{2,1,0:T(8,128)}) %reduce-scatter.10.cloned.1.call-update) | async-done | bytes 196624 | tf_op jit(solution)/shard_map/reduce_scatter | solution.py:63
  125.4 0.9 multiply_convert_fusion.2
  126.4 18.0 %all_to_all.15 = bf16[2,3,32,512]{3,2,1,0:T(8,128)(2,1)S(1)} all-to-all(bf16[2,3,32,512]{3,2,1,0:T(8,128)(2,1)S(1)} %pad_maximum_fusion.2), channel_id=1, replica_groups=mesh['z_hi'=2,'x'=4,'core'=2,'z_lo'=8,'y'=4] {'z_hi'}, dimensions={0} | all-to-all | bytes 393216 | tf_op jit(solution)/shard_map/all_to_all | solution.py:73
  144.4 1.0 stack.38
  145.3 4.8 %all-to-all-start.1 = ((bf16[4,3,64,512]{3,2,1,0:T(8,128)(2,1)}), bf16[4,3,64,512]{3,2,1,0:T(8,128)(2,1)S(1)}, u32[]{:S(2)}, u32[]{:S(2)}) async-start(bf16[4,3,64,512]{3,2,1,0:T(8,128)(2,1)} %stack.38), calls=%async_computation.4 | async-start | bytes 1572864 | tf_op jit(solution)/shard_map/all_to_all | solution.py:73
  150.1 0.0 reduce-scatter.12.cloned.1.call-start
  150.1 1.0 copy.29
  151.1 6.4 %all-to-all-done.1 = bf16[4,3,64,512]{3,2,1,0:T(8,128)(2,1)S(1)} async-done(((bf16[4,3,64,512]{3,2,1,0:T(8,128)(2,1)}), bf16[4,3,64,512]{3,2,1,0:T(8,128)(2,1)S(1)}, u32[]{:S(2)}, u32[]{:S(2)}) %all-to-all-start.1) | async-done | bytes 786464 | tf_op jit(solution)/shard_map/all_to_all | solution.py:73
  157.5 0.1 copy.27
  157.6 0.1 pad_maximum_fusion.1
  157.8 0.0 copy-start.3
  157.8 5.1 %all_to_all.16 = bf16[2,3,256,512]{3,2,1,0:T(8,128)(2,1)S(1)} all-to-all(bf16[2,3,256,512]{3,2,1,0:T(8,128)(2,1)S(1)} %pad_maximum_fusion.1), channel_id=1, replica_groups=mesh['z_hi'=2,'x'=4,'core'=2,'z_lo'=8,'y'=4] {'core'}, dimensions={0} | all-to-all | bytes 3145728 | tf_op jit(solution)/shard_map/all_to_all | solution.py:73
  162.9 0.9 fusion.3
  163.8 0.0 copy-done.3
  163.8 0.5 fusion.6
  164.3 0.0 copy-done.4
  164.3 1.5 convolution_add_fusion
  165.7 0.0 reduce-scatter.12.cloned.1.call-update
  165.7 0.2 reduce-scatter.14.cloned.1.call-start
  166.0 1.5 fusion.4
  167.4 2.5 abs.16
  169.9 2.8 %reduce_max.27 = f32[16,256]{0,1:T(8,128)S(1)} reduce(f32[16,32,256,2]{1,0,3,2:T(8,128)} %abs.16, f32[]{:T(128)} %constant.0.clone.1), dimensions={1,3}, to_apply=%region_5.0 | reduce | flops 258048 | bytes 1064964 | tf_op jit(solution)/shard_map/reduce_max | solution.py:17
  172.8 0.7 copy.33
  173.4 2.5 div.37
  176.0 3.6 %div.38 = f32[512,512]{0,1:T(8,128)S(1)} reshape(f32[16,32,256,2]{1,0,3,2:T(8,128)} %div.37) | data formatting | bytes 2097152 | tf_op jit(solution)/shard_map/div | solution.py:18
  179.6 1.0 divide_convert_fusion.2
  180.6 2.0 copy.32
  182.7 0.5 fusion.5
  183.1 2.5 abs.18
  185.6 2.8 %reduce_max.28 = f32[16,256]{0,1:T(8,128)S(1)} reduce(f32[16,32,256,2]{1,0,3,2:T(8,128)} %abs.18, f32[]{:T(128)} %constant.0.clone.1), dimensions={1,3}, to_apply=%region_6.0 | reduce | flops 258048 | bytes 1064964 | tf_op jit(solution)/shard_map/reduce_max | solution.py:17
  188.5 0.7 copy.35
  189.2 2.5 div.40
  191.7 3.5 %div.41 = f32[512,512]{0,1:T(8,128)S(1)} reshape(f32[16,32,256,2]{1,0,3,2:T(8,128)} %div.40) | data formatting | bytes 2097152 | tf_op jit(solution)/shard_map/div | solution.py:18
  195.3 0.2 divide_convert_fusion.1
  195.5 1.0 copy.34
  196.5 1.3 copy.28
  197.8 0.2 dot_general.46
  198.0 1.5 abs_reduce_fusion
  199.5 0.0 copy-start.6
  199.5 34.2 %reduce-scatter.12.cloned.1.call-done = f32[64,512]{1,0:T(8,128)} async-done(((f32[512,512]{1,0:T(8,128)}), f32[64,512]{1,0:T(8,128)}) %reduce-scatter.12.cloned.1.call-update) | async-done | bytes 131088 | tf_op jit(solution)/shard_map/reduce_scatter | solution.py:90
  233.7 0.0 reduce-scatter.14.cloned.1.call-update
  233.7 0.1 divide_convert_fusion
  233.9 3.0 %copy.31 = bf16[256,2,16,32]{3,2,1,0:T(8,128)(2,1)S(1)} copy(bf16[256,2,16,32]{0,3,2,1:T(8,128)(2,1)S(1)} %divide_convert_fusion) | data formatting | bytes 1048576 | tf_op jit(solution)/shard_map/convert_element_type | solution.py:27
  236.9 2.8 %convert_element_type.30 = bf16[512,512]{1,0:T(8,128)(2,1)} reshape(bf16[256,2,16,32]{3,2,1,0:T(8,128)(2,1)S(1)} %copy.31) | data formatting | bytes 1048576 | tf_op jit(solution)/shard_map/convert_element_type | solution.py:27
  239.6 0.0 copy-done.6
  239.6 19.1 %reduce-scatter.14.cloned.1.call-done = f32[16,512]{1,0:T(8,128)} async-done(((f32[64,512]{1,0:T(8,128)}), f32[16,512]{1,0:T(8,128)}) %reduce-scatter.14.cloned.1.call-update) | async-done | bytes 32784 | tf_op jit(solution)/shard_map/reduce_scatter | solution.py:91
  (9 shorter events, 0.1 us)
Async XLA Ops:
  7.2 1.0 copy-start
  7.2 4.0 %copy-start.2 = (bf16[512,512]{1,0:T(8,128)(2,1)S(1)}, bf16[512,512]{1,0:T(8,128)(2,1)}, u32[]{:S(2)}) copy-start(bf16[512,512]{1,0:T(8,128)(2,1)} %param.6) | copy-start | bytes 1572868
  7.2 4.0 %copy-start.5 = (bf16[512,512]{1,0:T(8,128)(2,1)S(1)}, bf16[512,512]{1,0:T(8,128)(2,1)}, u32[]{:S(2)}) copy-start(bf16[512,512]{1,0:T(8,128)(2,1)} %param.9) | copy-start | bytes 1572868
  7.2 32.6 %reduce-scatter.6.cloned.1.call-start = ((), (), s32[]{:S(2)}) async-start(), calls=%async_computation.8 | async-start | bytes 4718592 | tf_op jit(solution)/shard_map/reduce_scatter | solution.py:63
  13.6 62.9 %reduce-scatter.8.cloned.1.call-start = ((), (), s32[]{:S(2)}) async-start(), calls=%async_computation.9 | async-start | bytes 1966080 | tf_op jit(solution)/shard_map/reduce_scatter | solution.py:63
  39.8 85.5 %reduce-scatter.10.cloned.1.call-start = ((), (), s32[]{:S(2)}) async-start(), calls=%async_computation.10 | async-start | bytes 589824 | tf_op jit(solution)/shard_map/reduce_scatter | solution.py:63
  145.3 12.2 %all-to-all-start.1 = ((bf16[4,3,64,512]{3,2,1,0:T(8,128)(2,1)}), bf16[4,3,64,512]{3,2,1,0:T(8,128)(2,1)S(1)}, u32[]{:S(2)}, u32[]{:S(2)}) async-start(bf16[4,3,64,512]{3,2,1,0:T(8,128)(2,1)} %stack.38), calls=%async_computation.4 | async-start | bytes 1572864 | tf_op jit(solution)/shard_map/all_to_all | solution.py:73
  150.1 83.6 %reduce-scatter.12.cloned.1.call-start = ((), (), s32[]{:S(2)}) async-start(), calls=%async_computation.11 | async-start | bytes 1179648 | tf_op jit(solution)/shard_map/reduce_scatter | solution.py:90
  157.8 6.0 %copy-start.3 = (bf16[512,512]{1,0:T(8,128)(2,1)S(1)}, bf16[512,512]{1,0:T(8,128)(2,1)}, u32[]{:S(2)}) copy-start(bf16[512,512]{1,0:T(8,128)(2,1)} %param.7) | copy-start | bytes 1572868
  162.9 1.4 copy-start.4
  165.7 93.0 %reduce-scatter.14.cloned.1.call-start = ((), (), s32[]{:S(2)}) async-start(), calls=%async_computation.12 | async-start | bytes 163840 | tf_op jit(solution)/shard_map/reduce_scatter | solution.py:91
  176.0 3.6 %copy-start.1 = (f32[512,512]{0,1:T(8,128)S(1)}, f32[512,512]{0,1:T(8,128)}, u32[]{:S(2)}) copy-start(f32[512,512]{0,1:T(8,128)} %get-tuple-element.35) | copy-start | bytes 3145732
  199.5 40.1 %copy-start.6 = (f32[256,16]{0,1:T(8,128)}, f32[256,16]{0,1:T(8,128)S(1)}, u32[]{:S(2)}) copy-start(f32[256,16]{0,1:T(8,128)S(1)} %broadcast_add_fusion.2) | copy-start | bytes 49156
Sparse Core Ops, SparseCore 0:
  13.8 25.9 reduce-scatter.5
  42.6 33.8 reduce-scatter.7
  79.3 45.9 reduce-scatter.9
  165.9 67.8 reduce-scatter.11
  236.9 21.7 reduce-scatter.13
